TPU v7x, 32 devices: a whole 2x2x4 slice. The times are simulated.
32 devices in a mesh: req: 8 (over y, x, core), exp: 4 (over z).
Axes of the slice: x: 2, y: 2, z: 4, core: 2. Of those that a mesh axis runs over, the one named last changes fastest.
Arguments:
- tokens: bfloat16 [4096, 1024], P(('req', 'exp'))
- norm_attn: bfloat16 [1024], replicated, may hold values from 0.099609375 to 1.8984375
- w_query: bfloat16 [1024, 1024], replicated
- w_key: bfloat16 [1024, 512], replicated
- w_value: bfloat16 [1024, 512], replicated, may hold values from -0.1875 to 0.1875
- w_out: bfloat16 [1024, 1024], P('exp'), may hold values from -0.1875 to 0.1875
- norm_moe: bfloat16 [1024], replicated, may hold values from 0.099609375 to 1.8984375
- w_router: bfloat16 [1024, 32], replicated
- w_gate: bfloat16 [32, 1024, 512], P('exp'), may hold values from -0.1875 to 0.1875
- w_up: bfloat16 [32, 1024, 512], P('exp'), may hold values from -0.1875 to 0.1875
- w_down: bfloat16 [32, 512, 1024], P('exp')
- segment_ids: int32 [8, 512], P('req'), may hold values from 0 to 3, never falling along the last dimension, each value on 1 to 256 neighbouring positions
- page_order: int32 [8, 512], P('req'), may hold values from 0 to 511, each once within a row
- expert_ids: int32 [4096, 8], P(('req', 'exp')), may hold values from 0 to 31, all different within a row; in each aligned block of 128 rows (0 to 127, 128 to 255, ...) at most 64 rows name the same one
Outputs:
- mixed: bfloat16 [4096, 1024], P(('req', 'exp'))
- kv_cache: bfloat16 [4096, 8, 128], P('req', 'exp')
Inputs may be any that keep to these rules, and one draw needn't show every extreme that they name: `segment_ids`: along each row, request numbers never fall; every pack holds 4 requests of 1 to 256 positions, one of exactly 256. `page_order`: each row is a permutation of the pack's 512 positions. `expert_ids`: A token's 8 experts differ. Within the rows of one device no expert is named by more than 64 rows, and in some device's rows an expert is named by exactly 64.
All inputs are finite; a program needn't handle non-finite values.
Results may differ from a plain program's by a relative error of at most 0.0055.
Values may be sent and summed in bfloat16 or wider, within the bound.
No kernel may reach another device: no remote copies, remote signals or barrier semaphores. Data moves between devices by JAX's collectives and lax.ppermute only.
A program may use at most 128 MiB of HBM per device.

v0:
```python
import jax
import jax.numpy as jnp
from jax import lax
from jax.sharding import PartitionSpec as P

HD = 64
CAP = 64


def rms_scale(rows, gain):
    rows = rows.astype(jnp.float32)
    inverse = lax.rsqrt(jnp.mean(rows * rows, axis=-1, keepdims=True) + 1e-06)
    return (rows * inverse * gain.astype(jnp.float32)).astype(jnp.bfloat16)


def positions(seg):
    index = jnp.arange(seg.shape[0], dtype=jnp.int32)
    starts = jnp.concatenate([jnp.ones((1,), dtype=bool), seg[1:] != seg[:-1]])
    first = lax.cummax(jnp.where(starts, index, 0), axis=0)
    return index - first


def rotate(values, pos):
    half = values.shape[-1] // 2
    freq = 10000.0 ** (-jnp.arange(half, dtype=jnp.float32) / half)
    angle = pos.astype(jnp.float32)[:, None] * freq[None, :]
    cosine = jnp.cos(angle)[:, None, :]
    sine = jnp.sin(angle)[:, None, :]
    front = values[..., :half]
    back = values[..., half:]
    return jnp.concatenate([front * cosine - back * sine, back * cosine + front * sine], axis=-1)


def attend(query, keyval, seg):
    plen, groups, width = query.shape
    half = width // 2
    block = min(512, plen)
    blocks = plen // block
    queries = query.reshape(blocks, block, groups, 2, half)
    keys = keyval[..., :half]
    values = keyval[..., half:]
    key_pos = jnp.arange(plen, dtype=jnp.int32)
    query_pos = key_pos.reshape(blocks, block)
    query_seg = seg.reshape(blocks, block)

    def one_block(args):
        qblock, qpos, qseg = args
        score = (
            jnp.einsum("qkgd,tkd->kgqt", qblock, keys, preferred_element_type=jnp.float32) * 0.125
        )
        allowed = (qseg[:, None] == seg[None, :]) & (key_pos[None, :] <= qpos[:, None])
        score = jnp.where(allowed[None, None], score, -1e30)
        top = jnp.max(score, axis=-1, keepdims=True)
        expo = jnp.exp(score - top)
        probs = (expo / jnp.sum(expo, axis=-1, keepdims=True)).astype(jnp.bfloat16)
        out = jnp.einsum("kgqt,tkd->qkgd", probs, values, preferred_element_type=jnp.float32)
        return out.astype(jnp.bfloat16)

    outs = lax.map(one_block, (queries, query_pos, query_seg))
    return outs.reshape(plen, groups * width)


def expert_mix(rows_all, ids_all, w_router, w_gate, w_up, w_down):
    tokens_all = rows_all.shape[0]
    local = w_gate.shape[0]
    cap = CAP * lax.axis_size("exp")
    here = lax.axis_index("exp")
    logits = jnp.dot(rows_all, w_router, preferred_element_type=jnp.float32)
    weights = jax.nn.softmax(jnp.take_along_axis(logits, ids_all, axis=1), axis=-1)
    match = (ids_all - here * local)[:, :, None] == jnp.arange(local, dtype=jnp.int32)
    hits = jnp.any(match, axis=1)
    mine = jnp.sum(jnp.where(match, weights[:, :, None], 0.0), axis=1)
    order = jnp.arange(tokens_all, dtype=jnp.int32)
    before = (order[None, :] < order[:, None]).astype(jnp.bfloat16)
    slot = jnp.dot(before, hits.astype(jnp.bfloat16), preferred_element_type=jnp.float32)
    slot = slot.astype(jnp.int32)
    picks = hits.T[:, None, :] & (
        slot.T[:, None, :] == jnp.arange(cap, dtype=jnp.int32)[None, :, None]
    )
    received = jnp.einsum(
        "est,td->esd", picks.astype(jnp.bfloat16), rows_all, preferred_element_type=jnp.float32
    ).astype(jnp.bfloat16)
    gate = jnp.einsum("esd,edf->esf", received, w_gate, preferred_element_type=jnp.float32)
    upward = jnp.einsum("esd,edf->esf", received, w_up, preferred_element_type=jnp.float32)
    hidden = (jax.nn.silu(gate) * upward).astype(jnp.bfloat16)
    result = jnp.einsum("esf,efd->esd", hidden, w_down, preferred_element_type=jnp.float32)
    result = result.astype(jnp.bfloat16)
    combine = jnp.where(picks, mine.T[:, None, :], 0.0)
    high = combine.astype(jnp.bfloat16)
    low = (combine - high.astype(jnp.float32)).astype(jnp.bfloat16)
    partial = jnp.einsum("est,esd->td", high, result, preferred_element_type=jnp.float32)
    partial = partial + jnp.einsum("est,esd->td", low, result, preferred_element_type=jnp.float32)
    return partial


def shards(
    tokens,
    norm_attn,
    w_query,
    w_key,
    w_value,
    w_out,
    norm_moe,
    w_router,
    w_gate,
    w_up,
    w_down,
    segment_ids,
    page_order,
    expert_ids,
):
    rows, width = tokens.shape
    seg = segment_ids[0]
    groups = w_key.shape[1] // HD
    here = lax.axis_index("exp")
    ids_all = lax.all_gather(expert_ids, "exp", axis=0, tiled=True)
    pos = lax.dynamic_slice_in_dim(positions(seg), here * rows, rows)
    normed = rms_scale(tokens, norm_attn)
    query = jnp.dot(normed, w_query, preferred_element_type=jnp.float32).reshape(
        rows, 2 * groups, HD
    )
    query = rotate(query, pos).astype(jnp.bfloat16).reshape(rows, groups, 2 * HD)
    keys = jnp.dot(normed, w_key, preferred_element_type=jnp.float32).reshape(rows, groups, HD)
    keys = rotate(keys, pos).astype(jnp.bfloat16)
    values = (
        jnp.dot(normed, w_value, preferred_element_type=jnp.float32)
        .astype(jnp.bfloat16)
        .reshape(rows, groups, HD)
    )
    keyval = jnp.concatenate([keys, values], axis=-1)
    query_heads, keyval_heads = (
        lax.all_to_all(query, "exp", split_axis=1, concat_axis=0, tiled=True),
        lax.all_to_all(keyval, "exp", split_axis=1, concat_axis=0, tiled=True),
    )
    kv_cache = jnp.zeros_like(keyval_heads).at[page_order[0]].set(keyval_heads)
    heads_out = attend(query_heads, keyval_heads, seg)
    attention = lax.psum_scatter(
        jnp.dot(heads_out, w_out, preferred_element_type=jnp.float32),
        "exp",
        scatter_dimension=0,
        tiled=True,
    )
    resid = tokens.astype(jnp.float32) + attention
    normed2 = rms_scale(resid, norm_moe)
    rows_all = lax.all_gather(normed2, "exp", axis=0, tiled=True)
    partial = expert_mix(rows_all, ids_all, w_router, w_gate, w_up, w_down)
    moe = lax.psum_scatter(partial, "exp", scatter_dimension=0, tiled=True)
    mixed = (resid + moe).astype(jnp.bfloat16)
    return (mixed, kv_cache)


def solution(mesh):
    placed = (
        P(("req", "exp"), None),
        P(),
        P(),
        P(),
        P(),
        P("exp", None),
        P(),
        P(),
        P("exp", None, None),
        P("exp", None, None),
        P("exp", None, None),
        P("req", None),
        P("req", None),
        P(("req", "exp"), None),
    )
    return jax.shard_map(
        shards,
        mesh=mesh,
        in_specs=placed,
        out_specs=(P(("req", "exp"), None), P("req", "exp", None)),
        check_vma=False,
    )
```

profile of v0, /device:TPU:0, one launch (start us, length us, event | category | flops | bytes accessed | tf_op | source)
XLA Modules:
  0.0 250.5 jit_solution(3685987123882004109)
XLA Ops:
  7.2 0.9 compare_reduce_fusion
  8.2 1.1 fusion.31
  9.3 0.3 reduce-window.9
  9.7 0.1 slice_reduce_fusion
  9.9 0.7 convert_element_type.69
  10.6 1.7 convolution_convert_fusion.1
  12.3 0.1 copy.44
  12.4 1.9 fusion.49
  14.4 0.1 dynamic-slice_convert_fusion
  14.4 0.1 multiply_cosine_fusion
  14.6 0.7 pad_maximum_fusion
  15.4 6.3 %all-to-all-start = ((bf16[128,8,128]{0,2,1:T(8,128)(2,1)}), bf16[128,8,128]{0,2,1:T(8,128)(2,1)S(1)}, u32[]{:S(2)}, u32[]{:S(2)}) async-start(bf16[128,8,128]{0,2,1:T(8,128)(2,1)} %pad_maximum_fusion), calls=%async_computation | async-start | bytes 524288 | tf_op jit(solution)/shard_map/all_to_all | solution.py:133
  21.7 1.0 fusion.46
  22.8 0.7 pad_maximum_fusion.1
  23.5 7.1 %all-to-all-done = bf16[128,8,128]{0,2,1:T(8,128)(2,1)S(1)} async-done(((bf16[128,8,128]{0,2,1:T(8,128)(2,1)}), bf16[128,8,128]{0,2,1:T(8,128)(2,1)S(1)}, u32[]{:S(2)}, u32[]{:S(2)}) %all-to-all-start) | async-done | bytes 262176 | tf_op jit(solution)/shard_map/all_to_all | solution.py:133
  30.6 3.4 %all-to-all-start.1 = ((bf16[128,8,128]{0,2,1:T(8,128)(2,1)}), bf16[128,8,128]{0,2,1:T(8,128)(2,1)S(1)}, u32[]{:S(2)}, u32[]{:S(2)}) async-start(bf16[128,8,128]{0,2,1:T(8,128)(2,1)} %bitcast.12), calls=%async_computation.1 | async-start | bytes 524288 | tf_op jit(solution)/shard_map/all_to_all | solution.py:132
  34.1 0.2 fusion.30
  34.3 0.2 copy.62
  34.5 0.1 reshape.234
  34.6 6.4 %all-to-all-done.1 = bf16[128,8,128]{0,2,1:T(8,128)(2,1)S(1)} async-done(((bf16[128,8,128]{0,2,1:T(8,128)(2,1)}), bf16[128,8,128]{0,2,1:T(8,128)(2,1)S(1)}, u32[]{:S(2)}, u32[]{:S(2)}) %all-to-all-start.1) | async-done | bytes 262176 | tf_op jit(solution)/shard_map/all_to_all | solution.py:132
  41.0 0.2 copy.48
  41.2 0.1 squeeze.14
  41.3 3.6 %fusion.51 = (f32[2,2,512]{2,1,0:T(2,128)S(1)}, f32[2,2,512,512]{2,3,1,0:T(8,128)}) fusion(pred[512,512]{0,1:T(8,128)(4,1)S(1)} %fusion.30, bf16[512,2,2,64]{0,3,2,1:T(8,128)(2,1)S(1)} %squeeze.14, bf16[512,2,128]{0,2,1:T(8,128)(2,1)S(1)} %reshape.234), kind=kOutput, calls=%fused_computation.90 | convolution fusion | flops 138412544 | bytes 4857856 | tf_op jit(solution)/shard_map/while/body/eval_jaxpr/sub | solution.py:54
  44.9 2.7 %fusion.28 = bf16[2,64,2,512]{3,1,2,0:T(8,128)(2,1)S(1)} fusion(f32[2,2,512,512]{2,3,1,0:T(8,128)} %get-tuple-element.33, f32[2,2,512]{2,1,0:T(2,128)S(1)} %get-tuple-element.32, bf16[512,2,128]{0,2,1:T(8,128)(2,1)S(1)} %reshape.234), kind=kOutput, calls=%fused_computation.33 | convolution fusion | flops 136445952 | bytes 4595712 | tf_op jit(solution)/shard_map/while/body/eval_jaxpr/kgqt,tkd->qkgd/dot_general | solution.py:56
  47.7 1.8 fusion.52
  49.6 43.3 %reduce-scatter.3.cloned.1.call-done = f32[128,1024]{1,0:T(8,128)} async-done(((f32[512,1024]{1,0:T(8,128)}), f32[128,1024]{1,0:T(8,128)}) %reduce-scatter.3.cloned.1.call-update) | async-done | bytes 524304 | tf_op jit(solution)/shard_map/reduce_scatter | solution.py:137
  92.9 1.2 multiply_reduce_fusion
  94.1 1.9 multiply_convert_fusion.1
  96.1 13.3 %all_gather.6 = s32[512,8]{0,1:T(8,128)S(1)} all-gather(s32[128,8]{0,1:T(8,128)S(1)} %copy-done.11), channel_id=1, replica_groups=mesh['req'=8,'exp'=4] {'exp'}, dimensions={0}, use_global_device_ids=true | all-gather | bytes 20480 | tf_op jit(solution)/shard_map/all_gather | solution.py:116
  109.4 0.1 copy.50
  109.6 0.2 reshape.224
  109.8 0.9 convolution_convert_fusion.2
  110.6 12.8 %all-gather.2.cloned.1.call-done = bf16[512,1024]{1,0:T(8,128)(2,1)} async-done(((bf16[128,1024]{1,0:T(8,128)(2,1)}), bf16[512,1024]{1,0:T(8,128)(2,1)}) %all-gather.2.cloned.1.call-update) | async-done | bytes 1048592 | tf_op jit(solution)/shard_map/all_gather | solution.py:145
  123.4 1.6 fusion.53
  125.1 33.2 %gather_fusion = f32[4096]{0:T(1024)S(1)} fusion(f32[512,32]{0,1:T(8,128)S(1)} %fusion.53, s32[4096]{0:T(1024)S(1)} %reshape.224), kind=kCustom, calls=%fused_computation | custom fusion | bytes 65536 | tf_op jit(solution)/shard_map/jit(take_along_axis)/gather | solution.py:69
  158.3 0.9 reshape.227
  159.1 1.0 copy.51
  160.3 4.7 %fusion.6 = bf16[8,256,1024]{2,1,0:T(8,128)(2,1)S(1)} fusion(s32[8,512]{1,0:T(8,128)} %convolution_convert_fusion.2, pred[8,512]{1,0:T(8,128)(4,1)S(1)} %bitcast.100, bf16[512,1024]{1,0:T(8,128)(2,1)S(1)} %copy-done.5), kind=kOutput, calls=%fused_computation.15 | convolution fusion | flops 2151677952 | bytes 5263360 | tf_op jit(solution)/shard_map/est,td->esd/dot_general | solution.py:80
  165.1 2.0 copy-done.2
  167.0 7.7 %fusion.54 = f32[8,256,512]{2,1,0:T(8,128)} fusion(bf16[8,256,1024]{2,1,0:T(8,128)(2,1)S(1)} %fusion.6, bf16[8,1024,512]{2,1,0:T(8,128)(2,1)} %param.22), kind=kOutput, calls=%fused_computation.93 | convolution fusion | flops 2147483648 | bytes 16777216 | tf_op jit(solution)/shard_map/esd,edf->esf/dot_general | solution.py:83
  174.7 14.6 %convolution_convert_fusion = bf16[8,256,1024]{2,1,0:T(8,128)(2,1)} fusion(bf16[8,512,1024]{2,1,0:T(8,128)(2,1)} %param.24, f32[8,256,512]{2,1,0:T(8,128)} %fusion.54, bf16[8,256,1024]{2,1,0:T(8,128)(2,1)} %copy-done.2, bf16[8,1024,512]{2,1,0:T(8,128)(2,1)} %param.23), kind=kOutput, calls=%fused_computation.14 | convolution fusion | flops 4303355904 | bytes 29360128 | tf_op jit(solution)/shard_map/esf,efd->esd/dot_general | solution.py:86
  189.3 5.3 %fusion.9 = f32[512,1024,1]{1,0,2:T(8,128)S(1)} fusion(bf16[8,256,1024]{2,1,0:T(8,128)(2,1)} %convolution_convert_fusion, f32[8,512]{1,0:T(8,128)S(1)} %bitcast.97, s32[8,512]{1,0:T(8,128)S(1)} %copy-done.14, pred[8,512]{1,0:T(8,128)(4,1)S(1)} %bitcast.101), kind=kOutput, calls=%fused_computation.16 | convolution fusion | flops 2150629376 | bytes 6328320 | tf_op jit(solution)/shard_map/est,esd->td/dot_general | solution.py:91
  194.7 4.2 %bitcast_add_fusion = f32[512,1024]{1,0:T(8,128)} fusion(f32[512,1024,1]{1,0,2:T(8,128)S(1)} %fusion.9, bf16[8,256,1024]{2,1,0:T(8,128)(2,1)S(1)} %copy-done.15, f32[8,512]{1,0:T(8,128)S(1)} %bitcast.98, s32[8,512]{1,0:T(8,128)S(1)} %copy-done.14, pred[8,512]{1,0:T(8,128)(4,1)S(1)} %bitcast.102), kind=kOutput, calls=%fused_computation.18 | convolution fusion | flops 2155347968 | bytes 8425472 | tf_op jit(solution)/shard_map/est,esd->td/dot_general | solution.py:92
  198.9 0.2 copy.53
  199.1 0.1 broadcast_in_dim.101
  199.3 14.2 %scatter_fusion = bf16[512,2,128]{2,1,0:T(2,128)(2,1)S(1)} fusion(bf16[512,2,128]{2,1,0:T(2,128)(2,1)S(1)} %broadcast_in_dim.101, s32[512]{0:T(512)S(1)} %bitcast.99, bf16[512,2,128]{2,1,0:T(2,128)(2,1)S(1)} %copy.53), kind=kCustom, calls=%fused_computation.1 | custom fusion | bytes 788480 | tf_op jit(solution)/shard_map/scatter | solution.py:135
  213.5 28.6 %reduce-scatter.5.cloned.1.call-done = f32[128,1024]{1,0:T(8,128)} async-done(((f32[512,1024]{1,0:T(8,128)}), f32[128,1024]{1,0:T(8,128)}) %reduce-scatter.5.cloned.1.call-update) | async-done | bytes 524304 | tf_op jit(solution)/shard_map/reduce_scatter | solution.py:147
  242.1 1.8 add_convert_fusion
  (55 shorter events, 0.8 us)
Async XLA Ops:
  7.2 14.6 %copy-start = (bf16[1024,1024]{1,0:T(8,128)(2,1)S(1)}, bf16[1024,1024]{1,0:T(8,128)(2,1)}, u32[]{:S(2)}) copy-start(bf16[1024,1024]{1,0:T(8,128)(2,1)} %param.16) | copy-start | bytes 6291460
  7.2 14.5 %copy-start.1 = (bf16[128,1024]{1,0:T(8,128)(2,1)S(1)}, bf16[128,1024]{1,0:T(8,128)(2,1)}, u32[]{:S(2)}) copy-start(bf16[128,1024]{1,0:T(8,128)(2,1)} %param.14) | copy-start | bytes 786436
  12.3 21.8 %copy-start.10 = (s32[1,512]{1,0:T(1,128)S(1)}, s32[1,512]{1,0:T(1,128)}, u32[]{:S(2)}) copy-start(s32[1,512]{1,0:T(1,128)} %param.25) | copy-start | bytes 6148
  15.4 15.2 %all-to-all-start = ((bf16[128,8,128]{0,2,1:T(8,128)(2,1)}), bf16[128,8,128]{0,2,1:T(8,128)(2,1)S(1)}, u32[]{:S(2)}, u32[]{:S(2)}) async-start(bf16[128,8,128]{0,2,1:T(8,128)(2,1)} %pad_maximum_fusion), calls=%async_computation | async-start | bytes 524288 | tf_op jit(solution)/shard_map/all_to_all | solution.py:133
  30.6 10.4 %all-to-all-start.1 = ((bf16[128,8,128]{0,2,1:T(8,128)(2,1)}), bf16[128,8,128]{0,2,1:T(8,128)(2,1)S(1)}, u32[]{:S(2)}, u32[]{:S(2)}) async-start(bf16[128,8,128]{0,2,1:T(8,128)(2,1)} %bitcast.12), calls=%async_computation.1 | async-start | bytes 524288 | tf_op jit(solution)/shard_map/all_to_all | solution.py:132
  34.0 58.9 %reduce-scatter.3.cloned.1.call-start = ((), (), s32[]{:S(2)}) async-start(), calls=%async_computation.4 | async-start | bytes 2621440 | tf_op jit(solution)/shard_map/reduce_scatter | solution.py:137
  34.6 10.3 %copy-start.6 = (bf16[512,2,128]{0,2,1:T(8,128)(2,1)}, bf16[512,2,128]{0,2,1:T(8,128)(2,1)S(1)}, u32[]{:S(2)}) copy-start(bf16[512,2,128]{0,2,1:T(8,128)(2,1)S(1)} %reshape.234) | copy-start | bytes 786436
  44.9 2.8 %copy-start.8 = (bf16[256,1024]{1,0:T(8,128)(2,1)S(1)}, bf16[256,1024]{1,0:T(8,128)(2,1)}, u32[]{:S(2)}) copy-start(bf16[256,1024]{1,0:T(8,128)(2,1)} %param.19) | copy-start | bytes 1572868
  47.7 1.9 copy-start.12
  47.7 48.4 %copy-start.11 = (s32[128,8]{0,1:T(8,128)S(1)}, s32[128,8]{0,1:T(8,128)}, u32[]{:S(2)}) copy-start(s32[128,8]{0,1:T(8,128)} %param.27) | copy-start | bytes 12292
  47.7 75.7 %copy-start.9 = (bf16[1024,32]{0,1:T(8,128)(2,1)S(1)}, bf16[1024,32]{0,1:T(8,128)(2,1)}, u32[]{:S(2)}) copy-start(bf16[1024,32]{0,1:T(8,128)(2,1)} %param.21) | copy-start | bytes 196612
  49.5 73.9 %all-gather.2.cloned.1.call-start = ((), (), s32[]{:S(2)}) async-start(), calls=%async_computation.5 | async-start | bytes 1310720 | tf_op jit(solution)/shard_map/all_gather | solution.py:145
  96.0 146.1 %reduce-scatter.5.cloned.1.call-start = ((), (), s32[]{:S(2)}) async-start(), calls=%async_computation.6 | async-start | bytes 2621440 | tf_op jit(solution)/shard_map/reduce_scatter | solution.py:147
  125.0 35.3 %copy-start.5 = (bf16[512,1024]{1,0:T(8,128)(2,1)S(1)}, bf16[512,1024]{1,0:T(8,128)(2,1)}, u32[]{:S(2)}) copy-start(bf16[512,1024]{1,0:T(8,128)(2,1)} %all-gather.2.cloned.1.call-done) | copy-start | bytes 3145732
  165.0 2.0 copy-start.2
  174.7 14.6 %copy-start.14 = (s32[8,512]{1,0:T(8,128)S(1)}, s32[8,512]{1,0:T(8,128)}, u32[]{:S(2)}) copy-start(s32[8,512]{1,0:T(8,128)} %convolution_convert_fusion.2) | copy-start | bytes 49156
  189.3 5.3 %copy-start.15 = (bf16[8,256,1024]{2,1,0:T(8,128)(2,1)S(1)}, bf16[8,256,1024]{2,1,0:T(8,128)(2,1)}, u32[]{:S(2)}) copy-start(bf16[8,256,1024]{2,1,0:T(8,128)(2,1)} %convolution_convert_fusion) | copy-start | bytes 12582916
  194.6 4.3 %copy-start.13 = (s32[1,512]{1,0:T(1,128)S(1)}, s32[1,512]{1,0:T(1,128)}, u32[]{:S(2)}) copy-start(s32[1,512]{1,0:T(1,128)} %param.26) | copy-start | bytes 6148
  194.6 4.3 %copy-start.7 = (bf16[512,2,128]{0,2,1:T(8,128)(2,1)S(1)}, bf16[512,2,128]{0,2,1:T(8,128)(2,1)}, u32[]{:S(2)}) copy-start(bf16[512,2,128]{0,2,1:T(8,128)(2,1)} %copy-done.6) | copy-start | bytes 786436
  194.6 47.4 %copy-start.3 = (f32[128,1024]{1,0:T(8,128)S(1)}, f32[128,1024]{1,0:T(8,128)}, u32[]{:S(2)}) copy-start(f32[128,1024]{1,0:T(8,128)} %reduce-scatter.3.cloned.1.call-done) | copy-start | bytes 1572868
  213.5 30.5 %copy-start.4 = (bf16[512,2,128]{2,1,0:T(2,128)(2,1)}, bf16[512,2,128]{2,1,0:T(2,128)(2,1)S(1)}, u32[]{:S(2)}) copy-start(bf16[512,2,128]{2,1,0:T(2,128)(2,1)S(1)} %scatter_fusion) | copy-start | bytes 786436
Sparse Core Ops, SparseCore 0:
  49.7 43.2 reduce-scatter.2
  96.1 27.2 all-gather.1
  199.0 43.0 reduce-scatter.4
where the time goes:
time: 251 us; the launch traced here: 250 us
  waiting for transfers between devices  98.3 us (39%)
  local copies, waits for them, and re-layouts  52.9 us (21%)
  matrix products  51.7 us (21%)
  between operations  14.1 us (6%)
  blocking collectives  13.3 us (5%)
  other arithmetic  10.3 us (4%)
  starting transfers between devices  9.88 us (4%)
    reduce_scatter x1, waiting for transfers between devices, shards(): lax.psum_scatter(jnp.dot(heads_out, w_out, preferred_element_type=jnp.flo...  43.3 us
    gather x5, local copies, waits for them, and re-layouts, expert_mix(): jnp.take_along_axis(logits, ids_all, axis=1)  35.4 us
    reduce_scatter x1, waiting for transfers between devices, shards(): moe = lax.psum_scatter(partial, 'exp', scatter_dimension=0, tiled=True)  28.6 us
    dot_general x1, matrix products, expert_mix(): jnp.einsum('esf,efd->esd', hidden, w_down, preferred_element_type=jnp.flo...  14.6 us
    scatter x1, local copies, waits for them, and re-layouts, shards(): kv_cache = jnp.zeros_like(keyval_heads).at[page_order[0]].set(keyval_heads)  14.2 us
    all_gather x1, blocking collectives, shards(): ids_all = lax.all_gather(expert_ids, 'exp', axis=0, tiled=True)  13.3 us
    all_gather x1, waiting for transfers between devices, shards(): rows_all = lax.all_gather(normed2, 'exp', axis=0, tiled=True)  12.8 us
    dot_general x1, matrix products, expert_mix(): jnp.einsum('esd,edf->esf', received, w_gate, preferred_element_type=jnp.f...  7.68 us
  transfers between devices with their start and end apart: 5, of which 5 were waited for; matrix products, arithmetic and copies ran while one was open for 7% of the time, Pallas kernels for 0%

commit v1 on v0

--- a/solution.py
+++ b/solution.py
@@ -1,3 +1,4 @@
+import functools
 import jax
 import jax.numpy as jnp
 from jax import lax
@@ -5,6 +6,37 @@
 
 HD = 64
 CAP = 64
+
+
+def render_yards(w_in, array_axis, s0):
+    z = w_in.shape
+    return jnp.moveaxis(
+        w_in.reshape(*z[:array_axis], s0, z[array_axis] // s0, *z[array_axis + 1 :]), array_axis, 0
+    )
+
+
+def open_digits(arr, on_dim):
+    u_next = list(arr.shape[1:])
+    u_next[on_dim] *= arr.shape[0]
+    return jnp.moveaxis(arr, 0, on_dim).reshape(u_next)
+
+
+def _wait_packet(xx, row_axis, x_local, raw):
+    f_now = lax.psum(1, axis_name=row_axis)
+    finding = lax.axis_index(row_axis)
+    left_arr, y = (f_now, finding)
+    arr_next = render_yards(xx, x_local, left_arr)
+    pile = [arr_next[y]]
+    for s in [*range(1, left_arr)]:
+        clean = arr_next[y ^ s]
+        fresh = lax.ppermute(clean, axis_name=row_axis, perm=[(p, p ^ s) for p in range(left_arr)])
+        pile.append(fresh)
+    current_arr = jnp.stack(pile)
+    arr_next = current_arr[y ^ jnp.arange(left_arr)]
+    return open_digits(arr_next, raw)
+
+
+solve_flows = functools.partial(_wait_packet, row_axis="exp", x_local=1, raw=0)
 
 
 def rms_scale(rows, gain):
@@ -129,7 +161,7 @@
     )
     keyval = jnp.concatenate([keys, values], axis=-1)
     query_heads, keyval_heads = (
-        lax.all_to_all(query, "exp", split_axis=1, concat_axis=0, tiled=True),
+        solve_flows(query),
         lax.all_to_all(keyval, "exp", split_axis=1, concat_axis=0, tiled=True),
     )
     kv_cache = jnp.zeros_like(keyval_heads).at[page_order[0]].set(keyval_heads)

time: 251 us -> 248 us (0.988)
  waiting for transfers between devices: 98.3 us -> 91.6 us
    ppermute x0 -> x3, waiting for transfers between devices: none -> 7.33 us  [_wait_packet(): lax.ppermute(clean, axis_name=row_axis, perm=[(p, p ^ s) for p in range(l...]
    all_to_all x1, waiting for transfers between devices: 7.1 us -> 0.01 us  [shards(): lax.all_to_all(keyval, 'exp', split_axis=1, concat_axis=0, tiled=True)]
    all_to_all x1 -> x0, waiting for transfers between devices: 6.4 us -> none  [shards(): lax.all_to_all(query, 'exp', split_axis=1, concat_axis=0, tiled=True)]
    ppermute x0 -> x3, starting transfers between devices: none -> 4.6 us  [_wait_packet(): lax.ppermute(clean, axis_name=row_axis, perm=[(p, p ^ s) for p in range(l...]
    all_to_all x1 -> x0, starting transfers between devices: 3.41 us -> none  [shards(): lax.all_to_all(query, 'exp', split_axis=1, concat_axis=0, tiled=True)]
  transfers between devices with their start and end apart: 5 -> 7, of which waited for: 5 -> 5; matrix products, arithmetic and copies ran while one was open for 7% -> 8% of each run, Pallas kernels for 0% -> 0%
where the time goes in v1:
time: 248 us; the launch traced here: 247 us
  waiting for transfers between devices  91.6 us (37%)
  local copies, waits for them, and re-layouts  54.7 us (22%)
  matrix products  52.7 us (21%)
  between operations  14.2 us (6%)
  blocking collectives  13.3 us (5%)
  starting transfers between devices  11 us (4%)
  other arithmetic  9.6 us (4%)
    reduce_scatter x1, waiting for transfers between devices, shards(): lax.psum_scatter(jnp.dot(heads_out, w_out, preferred_element_type=jnp.flo...  42.8 us
    gather x5, local copies, waits for them, and re-layouts, expert_mix(): jnp.take_along_axis(logits, ids_all, axis=1)  35.4 us
    reduce_scatter x1, waiting for transfers between devices, shards(): moe = lax.psum_scatter(partial, 'exp', scatter_dimension=0, tiled=True)  28.6 us
    dot_general x1, matrix products, expert_mix(): jnp.einsum('esf,efd->esd', hidden, w_down, preferred_element_type=jnp.flo...  14.6 us
    scatter x1, local copies, waits for them, and re-layouts, shards(): kv_cache = jnp.zeros_like(keyval_heads).at[page_order[0]].set(keyval_heads)  14.2 us
    all_gather x1, blocking collectives, shards(): ids_all = lax.all_gather(expert_ids, 'exp', axis=0, tiled=True)  13.3 us
    all_gather x1, waiting for transfers between devices, shards(): rows_all = lax.all_gather(normed2, 'exp', axis=0, tiled=True)  12.9 us
    dot_general x1, matrix products, expert_mix(): jnp.einsum('esd,edf->esf', received, w_gate, preferred_element_type=jnp.f...  7.68 us
  transfers between devices with their start and end apart: 7, of which 5 were waited for; matrix products, arithmetic and copies ran while one was open for 8% of the time, Pallas kernels for 0%

profile of v1, /device:TPU:0, one launch (start us, length us, event | category | flops | bytes accessed | tf_op | source)
XLA Modules:
  0.0 247.1 jit_solution(5535986728086567876)
XLA Ops:
  7.2 0.9 compare_reduce_fusion
  8.2 1.1 fusion.31
  9.3 0.3 reduce-window.9
  9.9 0.7 convert_element_type.69
  10.6 1.7 convolution_convert_fusion.1
  12.4 1.9 fusion.50
  14.4 0.1 multiply_cosine_fusion
  14.6 0.7 pad_maximum_fusion
  15.4 6.4 %all-to-all-start = ((bf16[128,8,128]{0,2,1:T(8,128)(2,1)}), bf16[128,8,128]{0,2,1:T(8,128)(2,1)S(1)}, u32[]{:S(2)}, u32[]{:S(2)}) async-start(bf16[128,8,128]{0,2,1:T(8,128)(2,1)} %pad_maximum_fusion), calls=%async_computation | async-start | bytes 524288 | tf_op jit(solution)/shard_map/all_to_all | solution.py:165
  21.7 1.0 fusion.47
  22.9 0.1 copy.66
  23.0 2.1 collective-permute-start
  25.1 0.1 copy.67
  25.2 2.4 collective-permute-start.1
  27.8 0.2 fusion.30
  28.1 0.1 copy.65
  28.2 2.2 collective-permute-done
  30.4 5.1 %collective-permute-done.1 = bf16[128,2,128]{2,0,1:T(8,128)(2,1)S(1)} collective-permute-done((bf16[128,2,128]{2,0,1:T(8,128)(2,1)S(1)}, bf16[128,2,128]{2,0,1:T(8,128)(2,1)S(1)}, u32[]{:S(2)}, u32[]{:S(2)}) %collective-permute-start.1) | collective-permute-done | bytes 65568 | tf_op jit(solution)/shard_map/ppermute | solution.py:32
  35.6 0.6 gather_fusion
  36.2 0.2 copy.69
  36.4 0.8 squeeze.26
  37.2 0.2 copy.82
  37.5 4.6 %fusion.52 = (f32[2,2,512]{2,1,0:T(2,128)S(1)}, f32[2,2,512,512]{2,3,1,0:T(8,128)}) fusion(pred[512,512]{0,1:T(8,128)(4,1)S(1)} %fusion.30, bf16[512,2,2,64]{0,3,2,1:T(8,128)(2,1)} %squeeze.26, bf16[512,2,128]{0,2,1:T(8,128)(2,1)S(1)} %reshape.262), kind=kOutput, calls=%fused_computation.99 | convolution fusion | flops 138412544 | bytes 4857856 | tf_op jit(solution)/shard_map/while/body/eval_jaxpr/sub | solution.py:86
  42.2 2.7 %fusion.28 = bf16[2,64,2,512]{3,1,2,0:T(8,128)(2,1)S(1)} fusion(f32[2,2,512,512]{2,3,1,0:T(8,128)} %get-tuple-element.37, f32[2,2,512]{2,1,0:T(2,128)S(1)} %get-tuple-element.36, bf16[512,2,128]{0,2,1:T(8,128)(2,1)S(1)} %reshape.262), kind=kOutput, calls=%fused_computation.34 | convolution fusion | flops 136445952 | bytes 4595712 | tf_op jit(solution)/shard_map/while/body/eval_jaxpr/kgqt,tkd->qkgd/dot_general | solution.py:88
  44.9 1.8 fusion.53
  46.9 42.8 %reduce-scatter.3.cloned.1.call-done = f32[128,1024]{1,0:T(8,128)} async-done(((f32[512,1024]{1,0:T(8,128)}), f32[128,1024]{1,0:T(8,128)}) %reduce-scatter.3.cloned.1.call-update) | async-done | bytes 524304 | tf_op jit(solution)/shard_map/reduce_scatter | solution.py:169
  89.6 1.2 multiply_reduce_fusion
  90.8 1.9 multiply_convert_fusion.1
  92.8 13.3 %all_gather.6 = s32[512,8]{0,1:T(8,128)S(1)} all-gather(s32[128,8]{0,1:T(8,128)S(1)} %copy-done.11), channel_id=1, replica_groups=mesh['req'=8,'exp'=4] {'exp'}, dimensions={0}, use_global_device_ids=true | all-gather | bytes 20480 | tf_op jit(solution)/shard_map/all_gather | solution.py:148
  106.0 0.1 copy.71
  106.2 0.2 reshape.252
  106.4 0.9 convolution_convert_fusion.2
  107.2 12.9 %all-gather.2.cloned.1.call-done = bf16[512,1024]{1,0:T(8,128)(2,1)} async-done(((bf16[128,1024]{1,0:T(8,128)(2,1)}), bf16[512,1024]{1,0:T(8,128)(2,1)}) %all-gather.2.cloned.1.call-update) | async-done | bytes 1048592 | tf_op jit(solution)/shard_map/all_gather | solution.py:177
  120.1 1.6 fusion.54
  121.7 33.2 %gather_fusion.1 = f32[4096]{0:T(1024)S(1)} fusion(f32[512,32]{0,1:T(8,128)S(1)} %fusion.54, s32[4096]{0:T(1024)S(1)} %reshape.252), kind=kCustom, calls=%fused_computation.1 | custom fusion | bytes 65536 | tf_op jit(solution)/shard_map/jit(take_along_axis)/gather | solution.py:101
  155.0 0.9 reshape.255
  155.8 1.0 copy.72
  157.0 4.7 %fusion.6 = bf16[8,256,1024]{2,1,0:T(8,128)(2,1)S(1)} fusion(s32[8,512]{1,0:T(8,128)} %convolution_convert_fusion.2, pred[8,512]{1,0:T(8,128)(4,1)S(1)} %bitcast.113, bf16[512,1024]{1,0:T(8,128)(2,1)S(1)} %copy-done.5), kind=kOutput, calls=%fused_computation.16 | convolution fusion | flops 2151677952 | bytes 5263360 | tf_op jit(solution)/shard_map/est,td->esd/dot_general | solution.py:112
  161.7 2.0 copy-done.2
  163.7 7.7 %fusion.55 = f32[8,256,512]{2,1,0:T(8,128)} fusion(bf16[8,256,1024]{2,1,0:T(8,128)(2,1)S(1)} %fusion.6, bf16[8,1024,512]{2,1,0:T(8,128)(2,1)} %param.22), kind=kOutput, calls=%fused_computation.102 | convolution fusion | flops 2147483648 | bytes 16777216 | tf_op jit(solution)/shard_map/esd,edf->esf/dot_general | solution.py:115
  171.4 14.6 %convolution_convert_fusion = bf16[8,256,1024]{2,1,0:T(8,128)(2,1)} fusion(bf16[8,512,1024]{2,1,0:T(8,128)(2,1)} %param.24, f32[8,256,512]{2,1,0:T(8,128)} %fusion.55, bf16[8,256,1024]{2,1,0:T(8,128)(2,1)} %copy-done.2, bf16[8,1024,512]{2,1,0:T(8,128)(2,1)} %param.23), kind=kOutput, calls=%fused_computation.15 | convolution fusion | flops 4303355904 | bytes 29360128 | tf_op jit(solution)/shard_map/esf,efd->esd/dot_general | solution.py:118
  186.0 5.3 %fusion.9 = f32[512,1024,1]{1,0,2:T(8,128)S(1)} fusion(bf16[8,256,1024]{2,1,0:T(8,128)(2,1)} %convolution_convert_fusion, f32[8,512]{1,0:T(8,128)S(1)} %bitcast.110, s32[8,512]{1,0:T(8,128)S(1)} %copy-done.14, pred[8,512]{1,0:T(8,128)(4,1)S(1)} %bitcast.114), kind=kOutput, calls=%fused_computation.17 | convolution fusion | flops 2150629376 | bytes 6328320 | tf_op jit(solution)/shard_map/est,esd->td/dot_general | solution.py:123
  191.3 4.2 %bitcast_add_fusion = f32[512,1024]{1,0:T(8,128)} fusion(f32[512,1024,1]{1,0,2:T(8,128)S(1)} %fusion.9, bf16[8,256,1024]{2,1,0:T(8,128)(2,1)S(1)} %copy-done.15, f32[8,512]{1,0:T(8,128)S(1)} %bitcast.111, s32[8,512]{1,0:T(8,128)S(1)} %copy-done.14, pred[8,512]{1,0:T(8,128)(4,1)S(1)} %bitcast.115), kind=kOutput, calls=%fused_computation.19 | convolution fusion | flops 2155347968 | bytes 8425472 | tf_op jit(solution)/shard_map/est,esd->td/dot_general | solution.py:124
  195.6 0.2 copy.74
  195.8 0.1 broadcast_in_dim.102
  196.0 14.2 %scatter_fusion = bf16[512,2,128]{2,1,0:T(2,128)(2,1)S(1)} fusion(bf16[512,2,128]{2,1,0:T(2,128)(2,1)S(1)} %broadcast_in_dim.102, s32[512]{0:T(512)S(1)} %bitcast.112, bf16[512,2,128]{2,1,0:T(2,128)(2,1)S(1)} %copy.74), kind=kCustom, calls=%fused_computation.2 | custom fusion | bytes 788480 | tf_op jit(solution)/shard_map/scatter | solution.py:167
  210.2 28.6 %reduce-scatter.5.cloned.1.call-done = f32[128,1024]{1,0:T(8,128)} async-done(((f32[512,1024]{1,0:T(8,128)}), f32[128,1024]{1,0:T(8,128)}) %reduce-scatter.5.cloned.1.call-update) | async-done | bytes 524304 | tf_op jit(solution)/shard_map/reduce_scatter | solution.py:179
  238.8 1.8 add_convert_fusion
  (68 shorter events, 1.5 us)
Async XLA Ops:
  7.2 14.6 %copy-start = (bf16[1024,1024]{1,0:T(8,128)(2,1)S(1)}, bf16[1024,1024]{1,0:T(8,128)(2,1)}, u32[]{:S(2)}) copy-start(bf16[1024,1024]{1,0:T(8,128)(2,1)} %param.16) | copy-start | bytes 6291460
  7.2 14.5 %copy-start.1 = (bf16[128,1024]{1,0:T(8,128)(2,1)S(1)}, bf16[128,1024]{1,0:T(8,128)(2,1)}, u32[]{:S(2)}) copy-start(bf16[128,1024]{1,0:T(8,128)(2,1)} %param.14) | copy-start | bytes 786436
  12.4 15.4 %copy-start.10 = (s32[1,512]{1,0:T(1,128)S(1)}, s32[1,512]{1,0:T(1,128)}, u32[]{:S(2)}) copy-start(s32[1,512]{1,0:T(1,128)} %param.25) | copy-start | bytes 6148
  15.4 21.8 %all-to-all-start = ((bf16[128,8,128]{0,2,1:T(8,128)(2,1)}), bf16[128,8,128]{0,2,1:T(8,128)(2,1)S(1)}, u32[]{:S(2)}, u32[]{:S(2)}) async-start(bf16[128,8,128]{0,2,1:T(8,128)(2,1)} %pad_maximum_fusion), calls=%async_computation | async-start | bytes 524288 | tf_op jit(solution)/shard_map/all_to_all | solution.py:165
  21.7 67.9 %reduce-scatter.3.cloned.1.call-start = ((), (), s32[]{:S(2)}) async-start(), calls=%async_computation.3 | async-start | bytes 2621440 | tf_op jit(solution)/shard_map/reduce_scatter | solution.py:169
  23.0 7.4 %collective-permute-start = (bf16[128,2,128]{2,0,1:T(8,128)(2,1)S(1)}, bf16[128,2,128]{2,0,1:T(8,128)(2,1)S(1)}, u32[]{:S(2)}, u32[]{:S(2)}) collective-permute-start(bf16[128,2,128]{2,0,1:T(8,128)(2,1)S(1)} %bitcast.103), channel_id=1, source_target_pairs={{0,1},{1,0},{2,3},{3,2},{4,5},{5,4},{6,7},{7,6},{8,9},{9,8},{10,11... | collective-permute-start | bytes 196616 | tf_op jit(solution)/shard_map/ppermute | solution.py:32
  25.2 10.3 %collective-permute-start.1 = (bf16[128,2,128]{2,0,1:T(8,128)(2,1)S(1)}, bf16[128,2,128]{2,0,1:T(8,128)(2,1)S(1)}, u32[]{:S(2)}, u32[]{:S(2)}) collective-permute-start(bf16[128,2,128]{2,0,1:T(8,128)(2,1)S(1)} %bitcast.104), channel_id=1, source_target_pairs={{0,2},{1,3},{2,0},{3,1},{4,6},{5,7},{6,4},{7,5},{8,10},{9,11},{10,... | collective-permute-start | bytes 196616 | tf_op jit(solution)/shard_map/ppermute | solution.py:32
  27.8 7.8 %collective-permute-start.2 = (bf16[128,2,128]{2,0,1:T(8,128)(2,1)S(1)}, bf16[128,2,128]{2,0,1:T(8,128)(2,1)S(1)}, u32[]{:S(2)}, u32[]{:S(2)}) collective-permute-start(bf16[128,2,128]{2,0,1:T(8,128)(2,1)S(1)} %bitcast.105), channel_id=1, source_target_pairs={{0,3},{1,2},{2,1},{3,0},{4,7},{5,6},{6,5},{7,4},{8,11},{9,10},{10,... | collective-permute-start | bytes 196616 | tf_op jit(solution)/shard_map/ppermute | solution.py:32
  37.5 7.4 %copy-start.6 = (bf16[512,2,128]{0,2,1:T(8,128)(2,1)}, bf16[512,2,128]{0,2,1:T(8,128)(2,1)S(1)}, u32[]{:S(2)}) copy-start(bf16[512,2,128]{0,2,1:T(8,128)(2,1)S(1)} %reshape.262) | copy-start | bytes 786436
  42.1 2.8 %copy-start.8 = (bf16[256,1024]{1,0:T(8,128)(2,1)S(1)}, bf16[256,1024]{1,0:T(8,128)(2,1)}, u32[]{:S(2)}) copy-start(bf16[256,1024]{1,0:T(8,128)(2,1)} %param.19) | copy-start | bytes 1572868
  44.9 1.9 copy-start.12
  44.9 47.8 %copy-start.11 = (s32[128,8]{0,1:T(8,128)S(1)}, s32[128,8]{0,1:T(8,128)}, u32[]{:S(2)}) copy-start(s32[128,8]{0,1:T(8,128)} %param.27) | copy-start | bytes 12292
  44.9 75.2 %copy-start.9 = (bf16[1024,32]{0,1:T(8,128)(2,1)S(1)}, bf16[1024,32]{0,1:T(8,128)(2,1)}, u32[]{:S(2)}) copy-start(bf16[1024,32]{0,1:T(8,128)(2,1)} %param.21) | copy-start | bytes 196612
  46.8 73.3 %all-gather.2.cloned.1.call-start = ((), (), s32[]{:S(2)}) async-start(), calls=%async_computation.4 | async-start | bytes 1310720 | tf_op jit(solution)/shard_map/all_gather | solution.py:177
  92.7 146.1 %reduce-scatter.5.cloned.1.call-start = ((), (), s32[]{:S(2)}) async-start(), calls=%async_computation.5 | async-start | bytes 2621440 | tf_op jit(solution)/shard_map/reduce_scatter | solution.py:179
  121.7 35.3 %copy-start.5 = (bf16[512,1024]{1,0:T(8,128)(2,1)S(1)}, bf16[512,1024]{1,0:T(8,128)(2,1)}, u32[]{:S(2)}) copy-start(bf16[512,1024]{1,0:T(8,128)(2,1)} %all-gather.2.cloned.1.call-done) | copy-start | bytes 3145732
  161.7 2.0 copy-start.2
  171.4 14.6 %copy-start.14 = (s32[8,512]{1,0:T(8,128)S(1)}, s32[8,512]{1,0:T(8,128)}, u32[]{:S(2)}) copy-start(s32[8,512]{1,0:T(8,128)} %convolution_convert_fusion.2) | copy-start | bytes 49156
  186.0 5.3 %copy-start.15 = (bf16[8,256,1024]{2,1,0:T(8,128)(2,1)S(1)}, bf16[8,256,1024]{2,1,0:T(8,128)(2,1)}, u32[]{:S(2)}) copy-start(bf16[8,256,1024]{2,1,0:T(8,128)(2,1)} %convolution_convert_fusion) | copy-start | bytes 12582916
  191.3 4.3 %copy-start.13 = (s32[1,512]{1,0:T(1,128)S(1)}, s32[1,512]{1,0:T(1,128)}, u32[]{:S(2)}) copy-start(s32[1,512]{1,0:T(1,128)} %param.26) | copy-start | bytes 6148
  191.3 4.3 %copy-start.7 = (bf16[512,2,128]{0,2,1:T(8,128)(2,1)S(1)}, bf16[512,2,128]{0,2,1:T(8,128)(2,1)}, u32[]{:S(2)}) copy-start(bf16[512,2,128]{0,2,1:T(8,128)(2,1)} %copy-done.6) | copy-start | bytes 786436
  191.3 47.4 %copy-start.3 = (f32[128,1024]{1,0:T(8,128)S(1)}, f32[128,1024]{1,0:T(8,128)}, u32[]{:S(2)}) copy-start(f32[128,1024]{1,0:T(8,128)} %reduce-scatter.3.cloned.1.call-done) | copy-start | bytes 1572868
  210.2 30.5 %copy-start.4 = (bf16[512,2,128]{2,1,0:T(2,128)(2,1)}, bf16[512,2,128]{2,1,0:T(2,128)(2,1)S(1)}, u32[]{:S(2)}) copy-start(bf16[512,2,128]{2,1,0:T(2,128)(2,1)S(1)} %scatter_fusion) | copy-start | bytes 786436
Sparse Core Ops, SparseCore 0:
  46.9 42.6 reduce-scatter.2
  92.8 27.2 all-gather.1
  195.7 43.0 reduce-scatter.4
